TPU v7x, 256 devices: a whole 4x4x8 slice. The times are simulated.
256 devices in a mesh: blk: 32 (over y, z), tp: 8 (over x, core).
Axes of the slice: x: 4, y: 4, z: 8, core: 2. Of those that a mesh axis runs over, the one named last changes fastest.
Arguments:
- queries: bfloat16 [32768, 1664], P(('blk', 'tp')), may hold values from -120 to 120
- keys: bfloat16 [32768, 1664], P(('blk', 'tp')), may hold values from -6 to 6
- values: bfloat16 [32768, 1664], P(('blk', 'tp')), may hold values from -6 to 6
- segment_ids: int32 [32768], replicated, may hold values from -1 to 31, as said below
- proj_weight: bfloat16 [6656, 3072], P(None, 'tp'), may hold values from -0.078125 to 0.078125
Outputs:
- normed: bfloat16 [8192, 3072], P('blk', 'tp')
- seg_peaks: float32 [32], replicated
Inputs may be any that keep to these rules, and one draw needn't show every extreme that they name: `segment_ids`: ids other than -1 never fall along the pack; every image 0 to 31 occurs as one run of tokens that starts at a multiple of 4 and has a multiple of 4 tokens, at most 1024; some image has exactly 1024; -1 marks padding tokens, which may stand between images.
All inputs are finite; a program needn't handle non-finite values.
Results may differ from a plain program's by a relative error of at most 0.0056.
Values may be sent and summed in bfloat16 or wider, within the bound.
No kernel may reach another device: no remote copies, remote signals or barrier semaphores. Data moves between devices by JAX's collectives and lax.ppermute only.
A program may use at most 128 MiB of HBM per device.

v0:
```python
import jax
import jax.numpy as jnp
from jax import lax
from jax.sharding import PartitionSpec as P

HEAD = 128
masked_score = -1e30
epsilon = 1e-06


def from_behind(x, axis, by):
    devices = lax.axis_size(axis)
    pairs = [(i, i + by) for i in range(devices) if 0 <= i + by < devices]
    return lax.ppermute(x, axis, pairs)


def key_scores(query_heads, key_heads):
    return jnp.einsum(
        "rhd,khd->hrk", query_heads, key_heads, preferred_element_type=jnp.float32
    ) * HEAD ** (-0.5)


def finish(scores, allowed, value_heads):
    scores = jnp.where(allowed[None], scores, masked_score)
    row_top = jnp.max(scores, axis=2, keepdims=True)
    exp_terms = jnp.where(allowed[None], jnp.exp(scores - row_top), 0.0)
    row_total = jnp.maximum(jnp.sum(exp_terms, axis=2), 1.0)
    weights = exp_terms.astype(jnp.bfloat16)
    mixed_out = jnp.einsum("hrk,khd->rhd", weights, value_heads, preferred_element_type=jnp.float32)
    return mixed_out / row_total.T[:, :, None]


def per_device(queries, keys, values, segment_ids, proj_weight):
    group_count = lax.axis_size("blk")
    group_index = lax.axis_index("blk")
    part_index = lax.axis_index("tp")
    row_count = queries.shape[0]
    width = queries.shape[1]
    heads_count = width // HEAD
    block_len = segment_ids.shape[0] // group_count
    own_begin = group_index * block_len
    query_segs = lax.dynamic_slice_in_dim(
        segment_ids, own_begin + part_index * row_count, row_count
    )
    own_keys, own_values = (
        lax.all_gather(keys, "tp", axis=0, tiled=True),
        lax.all_gather(values, "tp", axis=0, tiled=True),
    )
    before_keys, before_values = from_behind((own_keys, own_values), "blk", 1)
    after_keys, after_values = from_behind((own_keys, own_values), "blk", -1)

    def neighbor_segs(offset):
        target = group_index + offset
        inside = (target >= 0) & (target < group_count)
        begin_at = jnp.clip(target, 0, group_count - 1) * block_len
        return jnp.where(inside, lax.dynamic_slice_in_dim(segment_ids, begin_at, block_len), -2)

    seg_sets = (neighbor_segs(-1), neighbor_segs(0), neighbor_segs(1))
    key_sets = (before_keys, own_keys, after_keys)
    masks = [
        (query_segs[:, None] == key_segs[None, :]) & (query_segs[:, None] >= 0)
        for key_segs in seg_sets
    ]
    query_heads = queries.reshape(row_count, heads_count, HEAD)
    all_keys = jnp.concatenate(key_sets, axis=0).reshape(3 * block_len, heads_count, HEAD)
    scores = key_scores(query_heads, all_keys)
    full_mask = jnp.concatenate(masks, axis=1)
    value_heads = jnp.concatenate((before_values, own_values, after_values), axis=0).reshape(
        3 * block_len, heads_count, HEAD
    )
    attended = finish(scores, full_mask, value_heads).reshape(row_count, width).astype(jnp.bfloat16)
    merged = attended.reshape(row_count // 4, 4 * width)
    projected = jnp.dot(
        lax.all_gather(merged, "tp", axis=0, tiled=True),
        proj_weight,
        preferred_element_type=jnp.float32,
    )
    row_segs = lax.dynamic_slice_in_dim(segment_ids, own_begin, block_len)[::4]
    member = row_segs[:, None] == jnp.arange(group_count, dtype=jnp.int32)[None, :]
    squares = jnp.sum(projected * projected, axis=1)
    seg_sums = jnp.sum(jnp.where(member, squares[:, None], 0.0), axis=0)
    seg_counts = jnp.sum(member.astype(jnp.float32), axis=0) * projected.shape[1]
    row_peak = jnp.max(jnp.where(member, jnp.max(projected, axis=1)[:, None], masked_score), axis=0)
    seg_sums, seg_counts = lax.psum((seg_sums, seg_counts), ("blk", "tp"))
    row_peak = lax.pmax(row_peak, ("blk", "tp"))
    seg_scale = lax.rsqrt(seg_sums / seg_counts + epsilon)
    row_scale = jnp.sum(jnp.where(member, seg_scale[None, :], 0.0), axis=1)
    normed = (projected * row_scale[:, None]).astype(jnp.bfloat16)
    return (normed, row_peak * seg_scale)


def solution(mesh):
    in_specs = (
        P(("blk", "tp"), None),
        P(("blk", "tp"), None),
        P(("blk", "tp"), None),
        P(),
        P(None, "tp"),
    )
    out_specs = (P("blk", "tp"), P())
    return jax.shard_map(
        per_device, mesh=mesh, in_specs=in_specs, out_specs=out_specs, check_vma=False
    )
```

profile of v0, /device:TPU:1, one launch (start us, length us, event | category | flops | bytes accessed | tf_op | source)
XLA Modules:
  0.0 441.4 jit_solution(14741535118343284138)
XLA Ops:
  7.2 0.0 all-gather.6.cloned.1.call-start
  7.2 2.0 copy.18
  9.2 0.0 all-gather.6.cloned.1.call-update
  9.2 0.0 all-gather.4.cloned.1.call-start
  9.3 0.7 all-gather.4.cloned.1.call-update
  10.0 0.0 all-gather.8.cloned.1.call-start
  10.0 39.3 %all-gather.6.cloned.1.call-done = bf16[1024,1664]{0,1:T(8,128)(2,1)} async-done(((bf16[128,1664]{0,1:T(8,128)(2,1)}), bf16[1024,1664]{0,1:T(8,128)(2,1)}) %all-gather.6.cloned.1.call-update) | async-done | bytes 3407888 | tf_op jit(solution)/shard_map/all_gather | solution.py:46
  49.4 1.3 collective-permute-start.3
  50.6 5.8 %collective-permute-start.2 = (bf16[1024,1664]{0,1:T(8,128)(2,1)}, bf16[1024,1664]{0,1:T(8,128)(2,1)}, u32[]{:S(2)}, u32[]{:S(2)}) collective-permute-start(bf16[1024,1664]{0,1:T(8,128)(2,1)} %all-gather.6.cloned.1.call-done), channel_id=1, source_target_pairs={{0,8},{8,16},{16,24},{24,32},{32,40},{40,48},{48,56},{56,64},{64,7... | collective-permute-start | bytes 10223624 | tf_op jit(solution)/shard_map/ppermute | solution.py:14
  56.4 2.0 copy.19
  58.4 0.8 broadcast_compare_fusion
  59.1 0.8 fusion.21
  60.0 23.7 %all-gather.4.cloned.1.call-done = bf16[1024,1664]{1,0:T(8,128)(2,1)} async-done(((bf16[128,1664]{1,0:T(8,128)(2,1)}), bf16[1024,1664]{1,0:T(8,128)(2,1)}) %all-gather.4.cloned.1.call-update) | async-done | bytes 3407888 | tf_op jit(solution)/shard_map/all_gather | solution.py:47
  83.6 1.3 collective-permute-start.1
  84.9 5.9 %collective-permute-start = (bf16[1024,1664]{1,0:T(8,128)(2,1)}, bf16[1024,1664]{1,0:T(8,128)(2,1)}, u32[]{:S(2)}, u32[]{:S(2)}) collective-permute-start(bf16[1024,1664]{1,0:T(8,128)(2,1)} %all-gather.4.cloned.1.call-done), channel_id=1, source_target_pairs={{0,8},{8,16},{16,24},{24,32},{32,40},{40,48},{48,56},{56,64},{64,7... | collective-permute-start | bytes 10223624 | tf_op jit(solution)/shard_map/ppermute | solution.py:14
  90.8 0.7 compare_and_fusion.2
  91.5 0.8 pad_add_fusion
  92.2 34.3 %collective-permute-done.3 = bf16[1024,1664]{0,1:T(8,128)(2,1)S(1)} collective-permute-done((bf16[1024,1664]{0,1:T(8,128)(2,1)}, bf16[1024,1664]{0,1:T(8,128)(2,1)S(1)}, u32[]{:S(2)}, u32[]{:S(2)}) %collective-permute-start.3) | collective-permute-done | bytes 3407904 | tf_op jit(solution)/shard_map/ppermute | solution.py:14
  126.5 1.0 collective-permute-done.2
  127.5 7.9 %pad_maximum_fusion.1 = bf16[3072,1664]{0,1:T(8,128)(2,1)} fusion(bf16[1024,1664]{0,1:T(8,128)(2,1)S(1)} %collective-permute-done.3, bf16[1024,1664]{0,1:T(8,128)(2,1)} %all-gather.6.cloned.1.call-done, bf16[1024,1664]{0,1:T(8,128)(2,1)} %collective-permute-done.2), kind=kLoop, calls=%fused_computation.5 | loop fusion | flops 30670848 | bytes 20447232 | tf_op jit(solution)/shard_map/concatenate | solution.py:65
  135.4 0.0 copy-start
  135.4 17.8 %fusion.22 = (f32[13,128]{1,0:T(8,128)S(1)}, bf16[13,128,3072]{1,2,0:T(8,128)(2,1)}) fusion(pred[128,3072]{0,1:T(8,128)(4,1)} %pad_add_fusion, bf16[3072,13,128]{0,2,1:T(8,128)(2,1)} %bitcast.30, bf16[128,13,128]{0,2,1:T(8,128)(2,1)} %bitcast.32), kind=kOutput, calls=%fused_computation.37 | convolution fusion | flops 1339296768 | bytes 21273088 | tf_op jit(solution)/shard_map/sub | solution.py:26
  153.2 46.5 %collective-permute-done.1 = bf16[1024,1664]{1,0:T(8,128)(2,1)} collective-permute-done((bf16[1024,1664]{1,0:T(8,128)(2,1)}, bf16[1024,1664]{1,0:T(8,128)(2,1)}, u32[]{:S(2)}, u32[]{:S(2)}) %collective-permute-start.1) | collective-permute-done | bytes 3407904 | tf_op jit(solution)/shard_map/ppermute | solution.py:14
  199.7 0.9 collective-permute-done
  200.5 0.0 copy-done
  200.5 15.7 %pad_maximum_fusion = bf16[3072,1664]{1,0:T(8,128)(2,1)} fusion(bf16[1024,1664]{1,0:T(8,128)(2,1)} %collective-permute-done.1, bf16[1024,1664]{1,0:T(8,128)(2,1)S(1)} %copy-done, bf16[1024,1664]{1,0:T(8,128)(2,1)} %collective-permute-done), kind=kLoop, calls=%fused_computation.4 | loop fusion | flops 30670848 | bytes 20447232 | tf_op jit(solution)/shard_map/concatenate | solution.py:68
  216.2 14.3 %copy.17 = bf16[3072,1664]{0,1:T(8,128)(2,1)} copy(bf16[3072,1664]{1,0:T(8,128)(2,1)} %pad_maximum_fusion) | data formatting | bytes 20447232 | tf_op jit(solution)/shard_map/concatenate | solution.py:68
  230.6 9.6 %fusion.15 = bf16[128,13,128]{0,2,1:T(8,128)(2,1)S(1)} fusion(bf16[3072,13,128]{0,2,1:T(8,128)(2,1)} %bitcast.31, bf16[13,128,3072]{1,2,0:T(8,128)(2,1)} %get-tuple-element.20, f32[128,13]{0,1:T(8,128)S(1)} %maximum_bitcast_fusion), kind=kOutput, calls=%fused_computation.15 | convolution fusion | flops 1309048832 | bytes 20879872 | tf_op jit(solution)/shard_map/hrk,khd->rhd/dot_general | solution.py:29
  240.2 0.4 copy.23
  240.6 1.1 convert_element_type.18
  241.7 0.0 all-gather.8.cloned.1.call-update
  241.7 0.2 slice.3
  241.9 35.6 %all-gather.8.cloned.1.call-done = bf16[256,6656]{1,0:T(8,128)(2,1)} async-done(((bf16[32,6656]{1,0:T(8,128)(2,1)}), bf16[256,6656]{1,0:T(8,128)(2,1)}) %all-gather.8.cloned.1.call-update) | async-done | bytes 3407888 | tf_op jit(solution)/shard_map/all_gather | solution.py:74
  277.5 5.5 %fusion.20 = (f32[256]{0:T(256)S(1)}, f32[256]{0:T(256)S(1)}, f32[256,384]{1,0:T(8,128)S(1)}) fusion(bf16[256,6656]{1,0:T(8,128)(2,1)} %all-gather.8.cloned.1.call-done, bf16[6656,384]{1,0:T(8,128)(2,1)} %param.9), kind=kOutput, calls=%fused_computation.35 | convolution fusion | flops 1308917248 | bytes 8914944 | tf_op jit(solution)/shard_map/dot_general | solution.py:73
  283.1 0.1 convert_reduce_fusion
  283.2 76.2 %all-reduce = (f32[32]{0:T(128)S(1)}, f32[32]{0:T(128)S(1)}) all-reduce(f32[32]{0:T(128)S(1)} %get-tuple-element.7, f32[32]{0:T(128)S(1)} %broadcast_multiply_fusion), channel_id=1, replica_groups=mesh['blk'=32,'tp'=8] {'blk','tp'}, use_global_device_ids=true, to_apply=%region_4.5 | all-reduce | flops 64 | bytes 512 | tf_op jit(solution)/shard_map/psum | solution.py:84
  359.5 0.1 select_reduce_fusion
  359.6 74.0 %pmax.7 = f32[32]{0:T(128)S(1)} all-reduce(f32[32]{0:T(128)S(1)} %get-tuple-element.4), channel_id=1, replica_groups=mesh['blk'=32,'tp'=8] {'blk','tp'}, use_global_device_ids=true, to_apply=%region_10.11 | all-reduce | flops 32 | bytes 256 | tf_op jit(solution)/shard_map/pmax | solution.py:85
  433.6 0.5 mul.57
  434.1 0.8 multiply_convert_fusion
  (3 shorter events, 0.0 us)
Async XLA Ops:
  7.2 42.2 %all-gather.6.cloned.1.call-start = ((), (), s32[]{:S(2)}) async-start(), calls=%async_computation.1 | async-start | bytes 3833856 | tf_op jit(solution)/shard_map/all_gather | solution.py:46
  9.2 74.4 %all-gather.4.cloned.1.call-start = ((), (), s32[]{:S(2)}) async-start(), calls=%async_computation | async-start | bytes 3833856 | tf_op jit(solution)/shard_map/all_gather | solution.py:47
  10.0 267.6 %all-gather.8.cloned.1.call-start = ((), (), s32[]{:S(2)}) async-start(), calls=%async_computation.2 | async-start | bytes 3833856 | tf_op jit(solution)/shard_map/all_gather | solution.py:74
  49.4 77.2 %collective-permute-start.3 = (bf16[1024,1664]{0,1:T(8,128)(2,1)}, bf16[1024,1664]{0,1:T(8,128)(2,1)S(1)}, u32[]{:S(2)}, u32[]{:S(2)}) collective-permute-start(bf16[1024,1664]{0,1:T(8,128)(2,1)} %all-gather.6.cloned.1.call-done), channel_id=1, source_target_pairs={{8,0},{16,8},{24,16},{32,24},{40,32},{48,40},{56,48},{64,56},{72,6... | collective-permute-start | bytes 10223624 | tf_op jit(solution)/shard_map/ppermute | solution.py:14
  50.6 76.8 %collective-permute-start.2 = (bf16[1024,1664]{0,1:T(8,128)(2,1)}, bf16[1024,1664]{0,1:T(8,128)(2,1)}, u32[]{:S(2)}, u32[]{:S(2)}) collective-permute-start(bf16[1024,1664]{0,1:T(8,128)(2,1)} %all-gather.6.cloned.1.call-done), channel_id=1, source_target_pairs={{0,8},{8,16},{16,24},{24,32},{32,40},{40,48},{48,56},{56,64},{64,7... | collective-permute-start | bytes 10223624 | tf_op jit(solution)/shard_map/ppermute | solution.py:14
  83.6 116.0 %collective-permute-start.1 = (bf16[1024,1664]{1,0:T(8,128)(2,1)}, bf16[1024,1664]{1,0:T(8,128)(2,1)}, u32[]{:S(2)}, u32[]{:S(2)}) collective-permute-start(bf16[1024,1664]{1,0:T(8,128)(2,1)} %all-gather.4.cloned.1.call-done), channel_id=1, source_target_pairs={{8,0},{16,8},{24,16},{32,24},{40,32},{48,40},{56,48},{64,56},{72,6... | collective-permute-start | bytes 10223624 | tf_op jit(solution)/shard_map/ppermute | solution.py:14
  84.9 115.6 %collective-permute-start = (bf16[1024,1664]{1,0:T(8,128)(2,1)}, bf16[1024,1664]{1,0:T(8,128)(2,1)}, u32[]{:S(2)}, u32[]{:S(2)}) collective-permute-start(bf16[1024,1664]{1,0:T(8,128)(2,1)} %all-gather.4.cloned.1.call-done), channel_id=1, source_target_pairs={{0,8},{8,16},{16,24},{24,32},{32,40},{40,48},{48,56},{56,64},{64,7... | collective-permute-start | bytes 10223624 | tf_op jit(solution)/shard_map/ppermute | solution.py:14
  135.4 65.1 %copy-start = (bf16[1024,1664]{1,0:T(8,128)(2,1)S(1)}, bf16[1024,1664]{1,0:T(8,128)(2,1)}, u32[]{:S(2)}) copy-start(bf16[1024,1664]{1,0:T(8,128)(2,1)} %all-gather.4.cloned.1.call-done) | copy-start | bytes 10223620
Sparse Core Ops, SparseCore 0:
  9.8 39.4 all-gather.5
  51.2 32.3 all-gather.3
  241.9 35.6 all-gather.7
where the time goes:
time: 442 us; the launch traced here: 441 us
  waiting for transfers between devices  182 us (41%)
  blocking collectives  150 us (34%)
  matrix products  32.9 us (7%)
  other arithmetic  28.2 us (6%)
  local copies, waits for them, and re-layouts  20 us (5%)
  starting transfers between devices  14.3 us (3%)
  between operations  13.8 us (3%)
    ppermute x4, waiting for transfers between devices, from_behind(): return lax.ppermute(x, axis, pairs)  82.6 us
    psum x1, blocking collectives, per_device(): seg_sums, seg_counts = lax.psum((seg_sums, seg_counts), ('blk', 'tp'))  76.2 us
    pmax x1, blocking collectives, per_device(): row_peak = lax.pmax(row_peak, ('blk', 'tp'))  74 us
    all_gather x1, waiting for transfers between devices, per_device(): lax.all_gather(keys, 'tp', axis=0, tiled=True)  39.3 us
    all_gather x1, waiting for transfers between devices, per_device(): lax.all_gather(merged, 'tp', axis=0, tiled=True)  35.6 us
    all_gather x1, waiting for transfers between devices, per_device(): lax.all_gather(values, 'tp', axis=0, tiled=True)  23.7 us
    sub x1, matrix products, finish(): exp_terms = jnp.where(allowed[None], jnp.exp(scores - row_top), 0.0)  17.8 us
    concatenate x1, other arithmetic, per_device(): jnp.concatenate((before_values, own_values, after_values), axis=0)  15.7 us
  transfers between devices with their start and end apart: 7, of which 7 were waited for; matrix products, arithmetic and copies ran while one was open for 7% of the time, Pallas kernels for 0%

commit v1 on v0

--- a/solution.py
+++ b/solution.py
@@ -44,7 +44,9 @@
     )
     own_keys, own_values = (
         lax.all_gather(keys, "tp", axis=0, tiled=True),
-        lax.all_gather(values, "tp", axis=0, tiled=True),
+        jnp.concatenate(
+            lax.all_to_all(jnp.stack([values] * lax.axis_size("tp")), "tp", 0, 0), axis=0
+        ),
     )
     before_keys, before_values = from_behind((own_keys, own_values), "blk", 1)
     after_keys, after_values = from_behind((own_keys, own_values), "blk", -1)

time: 442 us -> 465 us (1.052)
  blocking collectives: 150 us -> 210 us
  waiting for transfers between devices: 182 us -> 139 us
  local copies, waits for them, and re-layouts: 20 us -> 41.1 us
  other arithmetic: 28.2 us -> 12.5 us
    all_to_all x0 -> x1, blocking collectives: none -> 59.9 us  [per_device(): lax.all_to_all(jnp.stack([values] * lax.axis_size('tp')), 'tp', 0, 0)]
    all_gather x1, waiting for transfers between devices: 39.3 us -> 0.02 us  [per_device(): lax.all_gather(keys, 'tp', axis=0, tiled=True)]
    ppermute x4, waiting for transfers between devices: 82.6 us -> 107 us  [from_behind(): return lax.ppermute(x, axis, pairs)]
    all_gather x1 -> x0, waiting for transfers between devices: 23.7 us -> none  [per_device(): lax.all_gather(values, 'tp', axis=0, tiled=True)]
    concatenate x1 -> x0, other arithmetic: 15.7 us -> none  [per_device(): jnp.concatenate((before_values, own_values, after_values), axis=0)]
    all_to_all x0 -> x2, local copies, waits for them, and re-layouts: none -> 15 us  [per_device(): lax.all_to_all(jnp.stack([values] * lax.axis_size('tp')), 'tp', 0, 0)]
    ppermute x0 -> x2, local copies, waits for them, and re-layouts: none -> 11.1 us  [from_behind(): return lax.ppermute(x, axis, pairs)]
    concatenate x1, local copies, waits for them, and re-layouts: 14.3 us -> 6.61 us  [per_device(): jnp.concatenate((before_values, own_values, after_values), axis=0)]
  transfers between devices with their start and end apart: 7 -> 6, of which waited for: 7 -> 4; matrix products, arithmetic and copies ran while one was open for 7% -> 9% of each run, Pallas kernels for 0% -> 0%
where the time goes in v1:
time: 465 us; the launch traced here: 464 us
  blocking collectives  210 us (45%)
  waiting for transfers between devices  139 us (30%)
  local copies, waits for them, and re-layouts  41.1 us (9%)
  matrix products  32.9 us (7%)
  between operations  14.1 us (3%)
  starting transfers between devices  13.6 us (3%)
  other arithmetic  12.5 us (3%)
    ppermute x4, waiting for transfers between devices, from_behind(): return lax.ppermute(x, axis, pairs)  107 us
    psum x1, blocking collectives, per_device(): seg_sums, seg_counts = lax.psum((seg_sums, seg_counts), ('blk', 'tp'))  76.2 us
    pmax x1, blocking collectives, per_device(): row_peak = lax.pmax(row_peak, ('blk', 'tp'))  74 us
    all_to_all x1, blocking collectives, per_device(): lax.all_to_all(jnp.stack([values] * lax.axis_size('tp')), 'tp', 0, 0)  59.9 us
    all_gather x1, waiting for transfers between devices, per_device(): lax.all_gather(merged, 'tp', axis=0, tiled=True)  32.2 us
    sub x1, matrix products, finish(): exp_terms = jnp.where(allowed[None], jnp.exp(scores - row_top), 0.0)  17.9 us
    all_to_all x2, local copies, waits for them, and re-layouts, per_device(): lax.all_to_all(jnp.stack([values] * lax.axis_size('tp')), 'tp', 0, 0)  15 us
    ppermute x4, starting transfers between devices, from_behind(): return lax.ppermute(x, axis, pairs)  13.5 us
  transfers between devices with their start and end apart: 6, of which 4 were waited for; matrix products, arithmetic and copies ran while one was open for 9% of the time, Pallas kernels for 0%

profile of v1, /device:TPU:1, one launch (start us, length us, event | category | flops | bytes accessed | tf_op | source)
XLA Modules:
  0.0 463.6 jit_solution(8590219905536601422)
XLA Ops:
  7.2 0.0 all-gather.3.cloned.1.call-start
  7.2 2.0 copy.41
  9.2 0.0 all-gather.3.cloned.1.call-update
  9.2 0.0 all-gather.5.cloned.1.call-start
  9.3 1.3 copy.36
  10.5 0.4 stack.2
  11.0 59.9 %all_to_all.5 = bf16[8,128,1664]{1,2,0:T(8,128)(2,1)S(1)} all-to-all(bf16[8,128,1664]{1,2,0:T(8,128)(2,1)S(1)} %stack.2), channel_id=1, replica_groups=mesh['blk'=32,'tp'=8] {'tp'}, dimensions={0} | all-to-all | bytes 6815744 | tf_op jit(solution)/shard_map/all_to_all | solution.py:48
  70.8 4.1 copy.37
  74.9 5.2 %collective-permute-start = (bf16[1024,1664]{1,0:T(8,128)(2,1)}, bf16[1024,1664]{1,0:T(8,128)(2,1)}, u32[]{:S(2)}, u32[]{:S(2)}) collective-permute-start(bf16[1024,1664]{1,0:T(8,128)(2,1)} %bitcast.32), channel_id=1, source_target_pairs={{0,8},{8,16},{16,24},{24,32},{32,40},{40,48},{48,56},{56,64},{64,7... | collective-permute-start | bytes 10223624 | tf_op jit(solution)/shard_map/ppermute | solution.py:14
  80.1 1.3 collective-permute-start.1
  81.4 0.0 all-gather.3.cloned.1.call-done
  81.4 5.8 %collective-permute-start.2 = (bf16[1024,1664]{0,1:T(8,128)(2,1)}, bf16[1024,1664]{0,1:T(8,128)(2,1)}, u32[]{:S(2)}, u32[]{:S(2)}) collective-permute-start(bf16[1024,1664]{0,1:T(8,128)(2,1)} %all-gather.3.cloned.1.call-done), channel_id=1, source_target_pairs={{0,8},{8,16},{16,24},{24,32},{32,40},{40,48},{48,56},{56,64},{64,7... | collective-permute-start | bytes 10223624 | tf_op jit(solution)/shard_map/ppermute | solution.py:14
  87.2 1.3 collective-permute-start.3
  88.5 2.0 copy.42
  90.5 0.8 broadcast_compare_fusion
  91.3 0.8 fusion.27
  92.1 0.7 compare_and_fusion.2
  92.8 0.8 pad_add_fusion
  93.6 10.9 %copy.39 = bf16[8,128,1664]{1,0,2:T(8,128)(2,1)} copy(bf16[8,128,1664]{1,2,0:T(8,128)(2,1)S(1)} %all_to_all.5) | data formatting | bytes 6815744 | tf_op jit(solution)/shard_map/all_to_all | solution.py:48
  104.5 0.0 copy-start
  104.5 6.6 %concatenate.17 = bf16[1024,13,128]{0,2,1:T(8,128)(2,1)} reshape(bf16[8,128,1664]{1,0,2:T(8,128)(2,1)} %copy.39) | data formatting | bytes 6815744 | tf_op jit(solution)/shard_map/concatenate | solution.py:70
  111.1 39.6 %collective-permute-done = bf16[1024,1664]{1,0:T(8,128)(2,1)} collective-permute-done((bf16[1024,1664]{1,0:T(8,128)(2,1)}, bf16[1024,1664]{1,0:T(8,128)(2,1)}, u32[]{:S(2)}, u32[]{:S(2)}) %collective-permute-start) | collective-permute-done | bytes 3407904 | tf_op jit(solution)/shard_map/ppermute | solution.py:14
  150.7 5.6 %copy.38 = bf16[1024,1664]{0,1:T(8,128)(2,1)} copy(bf16[1024,1664]{1,0:T(8,128)(2,1)} %collective-permute-done) | data formatting | bytes 6815744 | tf_op jit(solution)/shard_map/ppermute | solution.py:14
  156.2 0.0 collective-permute-done.1
  156.2 5.6 %copy.40 = bf16[1024,1664]{0,1:T(8,128)(2,1)} copy(bf16[1024,1664]{1,0:T(8,128)(2,1)} %collective-permute-done.1) | data formatting | bytes 6815744 | tf_op jit(solution)/shard_map/ppermute | solution.py:14
  161.8 61.9 %collective-permute-done.2 = bf16[1024,1664]{0,1:T(8,128)(2,1)} collective-permute-done((bf16[1024,1664]{0,1:T(8,128)(2,1)}, bf16[1024,1664]{0,1:T(8,128)(2,1)}, u32[]{:S(2)}, u32[]{:S(2)}) %collective-permute-start.2) | collective-permute-done | bytes 3407904 | tf_op jit(solution)/shard_map/ppermute | solution.py:14
  223.7 5.5 %collective-permute-done.3 = bf16[1024,1664]{0,1:T(8,128)(2,1)} collective-permute-done((bf16[1024,1664]{0,1:T(8,128)(2,1)}, bf16[1024,1664]{0,1:T(8,128)(2,1)}, u32[]{:S(2)}, u32[]{:S(2)}) %collective-permute-start.3) | collective-permute-done | bytes 3407904 | tf_op jit(solution)/shard_map/ppermute | solution.py:14
  229.2 0.0 copy-done
  229.2 7.9 %pad_maximum_fusion = bf16[3072,1664]{0,1:T(8,128)(2,1)} fusion(bf16[1024,1664]{0,1:T(8,128)(2,1)} %collective-permute-done.3, bf16[1024,1664]{0,1:T(8,128)(2,1)S(1)} %copy-done, bf16[1024,1664]{0,1:T(8,128)(2,1)} %collective-permute-done.2), kind=kLoop, calls=%fused_computation.10 | loop fusion | flops 30670848 | bytes 20447232 | tf_op jit(solution)/shard_map/concatenate | solution.py:67
  237.2 0.0 copy-start.1
  237.2 17.9 %fusion.28 = (f32[13,128]{1,0:T(8,128)S(1)}, bf16[13,128,3072]{1,2,0:T(8,128)(2,1)}) fusion(pred[128,3072]{0,1:T(8,128)(4,1)} %pad_add_fusion, bf16[3072,13,128]{0,2,1:T(8,128)(2,1)} %bitcast.31, bf16[128,13,128]{0,2,1:T(8,128)(2,1)} %bitcast.36), kind=kOutput, calls=%fused_computation.41 | convolution fusion | flops 1339296768 | bytes 21273088 | tf_op jit(solution)/shard_map/sub | solution.py:26
  255.1 0.0 copy-done.1
  255.1 9.5 %divide_convert_fusion = bf16[128,13,128]{0,2,1:T(8,128)(2,1)} fusion(bf16[13,128,3072]{1,2,0:T(8,128)(2,1)} %get-tuple-element.20, bf16[1024,13,128]{0,2,1:T(8,128)(2,1)} %bitcast.35, bf16[1024,13,128]{0,2,1:T(8,128)(2,1)S(1)} %copy-done.1, bf16[1024,13,128]{0,2,1:T(8,128)(2,1)} %bitcast.34, f32[128,13]{0,1:T(8,128)S(1)} %maximum_bitcast_fusion), kind=kOutput, calls=%fused_computation.18 | convolution fusion | flops 1339719680 | bytes 20879872 | tf_op jit(solution)/shard_map/hrk,khd->rhd/dot_general | solution.py:29
  264.6 1.4 copy.46
  266.0 1.1 convert_element_type.18
  267.1 0.0 all-gather.5.cloned.1.call-update
  267.1 0.2 slice.3
  267.3 32.2 %all-gather.5.cloned.1.call-done = bf16[256,6656]{1,0:T(8,128)(2,1)} async-done(((bf16[32,6656]{1,0:T(8,128)(2,1)}), bf16[256,6656]{1,0:T(8,128)(2,1)}) %all-gather.5.cloned.1.call-update) | async-done | bytes 3407888 | tf_op jit(solution)/shard_map/all_gather | solution.py:76
  299.5 5.5 %fusion.26 = (f32[256]{0:T(256)S(1)}, f32[256]{0:T(256)S(1)}, f32[256,384]{1,0:T(8,128)S(1)}) fusion(bf16[256,6656]{1,0:T(8,128)(2,1)} %all-gather.5.cloned.1.call-done, bf16[6656,384]{1,0:T(8,128)(2,1)} %param.9), kind=kOutput, calls=%fused_computation.39 | convolution fusion | flops 1308917248 | bytes 8914944 | tf_op jit(solution)/shard_map/dot_general | solution.py:75
  305.0 0.1 convert_reduce_fusion
  305.2 76.2 %all-reduce = (f32[32]{0:T(128)S(1)}, f32[32]{0:T(128)S(1)}) all-reduce(f32[32]{0:T(128)S(1)} %get-tuple-element.7, f32[32]{0:T(128)S(1)} %broadcast_multiply_fusion), channel_id=1, replica_groups=mesh['blk'=32,'tp'=8] {'blk','tp'}, use_global_device_ids=true, to_apply=%region_4.5 | all-reduce | flops 64 | bytes 512 | tf_op jit(solution)/shard_map/psum | solution.py:86
  381.4 0.1 select_reduce_fusion
  381.5 74.0 %pmax.7 = f32[32]{0:T(128)S(1)} all-reduce(f32[32]{0:T(128)S(1)} %get-tuple-element.4), channel_id=1, replica_groups=mesh['blk'=32,'tp'=8] {'blk','tp'}, use_global_device_ids=true, to_apply=%region_10.11 | all-reduce | flops 32 | bytes 256 | tf_op jit(solution)/shard_map/pmax | solution.py:87
  455.5 0.5 mul.57
  456.0 0.8 multiply_convert_fusion
  (3 shorter events, 0.0 us)
Async XLA Ops:
  7.2 74.3 %all-gather.3.cloned.1.call-start = ((), (), s32[]{:S(2)}) async-start(), calls=%async_computation.1 | async-start | bytes 3833856 | tf_op jit(solution)/shard_map/all_gather | solution.py:46
  9.2 290.3 %all-gather.5.cloned.1.call-start = ((), (), s32[]{:S(2)}) async-start(), calls=%async_computation.2 | async-start | bytes 3833856 | tf_op jit(solution)/shard_map/all_gather | solution.py:76
  74.9 75.7 %collective-permute-start = (bf16[1024,1664]{1,0:T(8,128)(2,1)}, bf16[1024,1664]{1,0:T(8,128)(2,1)}, u32[]{:S(2)}, u32[]{:S(2)}) collective-permute-start(bf16[1024,1664]{1,0:T(8,128)(2,1)} %bitcast.32), channel_id=1, source_target_pairs={{0,8},{8,16},{16,24},{24,32},{32,40},{40,48},{48,56},{56,64},{64,7... | collective-permute-start | bytes 10223624 | tf_op jit(solution)/shard_map/ppermute | solution.py:14
  80.1 76.1 %collective-permute-start.1 = (bf16[1024,1664]{1,0:T(8,128)(2,1)}, bf16[1024,1664]{1,0:T(8,128)(2,1)}, u32[]{:S(2)}, u32[]{:S(2)}) collective-permute-start(bf16[1024,1664]{1,0:T(8,128)(2,1)} %bitcast.33), channel_id=1, source_target_pairs={{8,0},{16,8},{24,16},{32,24},{40,32},{48,40},{56,48},{64,56},{72,6... | collective-permute-start | bytes 10223624 | tf_op jit(solution)/shard_map/ppermute | solution.py:14
  81.4 142.3 %collective-permute-start.2 = (bf16[1024,1664]{0,1:T(8,128)(2,1)}, bf16[1024,1664]{0,1:T(8,128)(2,1)}, u32[]{:S(2)}, u32[]{:S(2)}) collective-permute-start(bf16[1024,1664]{0,1:T(8,128)(2,1)} %all-gather.3.cloned.1.call-done), channel_id=1, source_target_pairs={{0,8},{8,16},{16,24},{24,32},{32,40},{40,48},{48,56},{56,64},{64,7... | collective-permute-start | bytes 10223624 | tf_op jit(solution)/shard_map/ppermute | solution.py:14
  87.2 142.0 %collective-permute-start.3 = (bf16[1024,1664]{0,1:T(8,128)(2,1)}, bf16[1024,1664]{0,1:T(8,128)(2,1)}, u32[]{:S(2)}, u32[]{:S(2)}) collective-permute-start(bf16[1024,1664]{0,1:T(8,128)(2,1)} %all-gather.3.cloned.1.call-done), channel_id=1, source_target_pairs={{8,0},{16,8},{24,16},{32,24},{40,32},{48,40},{56,48},{64,56},{72,6... | collective-permute-start | bytes 10223624 | tf_op jit(solution)/shard_map/ppermute | solution.py:14
  104.5 124.8 %copy-start = (bf16[1024,1664]{0,1:T(8,128)(2,1)S(1)}, bf16[1024,1664]{0,1:T(8,128)(2,1)}, u32[]{:S(2)}) copy-start(bf16[1024,1664]{0,1:T(8,128)(2,1)} %all-gather.3.cloned.1.call-done) | copy-start | bytes 10223620
  237.2 18.0 %copy-start.1 = (bf16[1024,13,128]{0,2,1:T(8,128)(2,1)S(1)}, bf16[1024,13,128]{0,2,1:T(8,128)(2,1)}, u32[]{:S(2)}) copy-start(bf16[1024,13,128]{0,2,1:T(8,128)(2,1)} %concatenate.17) | copy-start | bytes 10223620
Sparse Core Ops, SparseCore 0:
  9.8 62.1 all-gather.2
  267.2 32.2 all-gather.4
